TPU v7x, 256 devices: a whole 4x4x8 slice. The times are simulated.
256 devices in a mesh: seq: 32 (over y, x, core), resp: 8 (over z).
Axes of the slice: x: 4, y: 4, z: 8, core: 2. Of those that a mesh axis runs over, the one named last changes fastest.
Arguments:
- prompt_grad: bfloat16 [32768, 4096], P('seq', 'resp'), may hold values from -0.119628906 to 0.119628906
- prompt_keys: bfloat16 [32768, 128], P('seq'), may hold values from -6 to 6
- prompt_queries: bfloat16 [32768, 128], P('seq'), may hold values from -0.52734375 to 0.52734375
- prompt_decay: float32 [64, 32768], P('resp', 'seq'), may hold values from -2 to 0
- resp_grad: bfloat16 [32768, 4096], P('resp', 'seq'), may hold values from -0.119628906 to 0.119628906
- resp_keys: bfloat16 [32768, 128], P('resp'), may hold values from -6 to 6
- resp_queries: bfloat16 [32768, 128], P('resp'), may hold values from -0.52734375 to 0.52734375
- resp_decay: float32 [64, 32768], P('seq', 'resp'), may hold values from -2 to 0
- resp_segment: int32 [32768], P('resp'), may hold values from 0 to 8, as said below
Outputs:
- prompt_dx: bfloat16 [32768, 4096], P('seq', 'resp')
- resp_dx: bfloat16 [32768, 4096], P('resp', 'seq')
Inputs may be any that keep to these rules, and one draw needn't show every extreme that they name: `resp_segment`: each aligned block of 4096 slots holds responses 0 to 7 in this order, each of one slot or more, then padding slots marked 8; a block holds 1024 live slots or more, and some block has no padding.
All inputs are finite; a program needn't handle non-finite values.
Results may differ from a plain program's by a relative error of at most 0.0057.
Values sent between devices are 32-bit elements; how exact they have to be, the bound alone decides.
No kernel may reach another device: no remote copies, remote signals or barrier semaphores. Data moves between devices by JAX's collectives and lax.ppermute only.
A program may use at most 64 MiB of HBM per device.

v0:
```python
import jax
import jax.numpy as jnp
from jax import lax
from jax.sharding import PartitionSpec as P

P_SIZE = 64
N = 128
GROUP = 256
RESP_DEV = 8


def group_parts(out_grad, queries, decay, segment, alive_mask):
    tokens = out_grad.shape[0]
    head_count = decay.shape[0]
    groups = tokens // GROUP
    cum_sums = jnp.cumsum(decay, axis=1)
    cum_group = cum_sums.reshape(head_count, groups, GROUP).transpose(1, 0, 2)
    decay_group = decay.reshape(head_count, groups, GROUP).transpose(1, 0, 2)
    before = cum_group[:, :, 0] - decay_group[:, :, 0]
    seg_group = segment.reshape(groups, GROUP)
    alive_group = alive_mask.reshape(groups, GROUP)
    first_label = seg_group[:, 0]
    last_label = seg_group[:, -1]
    grad_group = out_grad.reshape(groups, GROUP, head_count, P_SIZE)
    query_group = queries.reshape(groups, GROUP, N)
    keep_mask = (seg_group == first_label[:, None]) & alive_group
    factor = jnp.where(keep_mask[:, None, :], jnp.exp(cum_group - before[:, :, None]), 0.0)
    weighted = (factor.transpose(0, 2, 1)[:, :, :, None] * grad_group).astype(jnp.bfloat16)
    states = jnp.einsum("clhp,cln->chpn", weighted, query_group, preferred_element_type=jnp.float32)
    group_gains = jnp.exp(cum_group[:, :, -1] - before)
    joined = (first_label == last_label).astype(jnp.float32)
    linked = jnp.concatenate(
        [jnp.ones((1,), jnp.float32), (last_label[:-1] == first_label[1:]).astype(jnp.float32)]
    )
    flow = (
        joined[:, None]
        * group_gains
        * jnp.concatenate([linked[1:], jnp.zeros((1,), jnp.float32)])[:, None]
    )
    carry_at = jnp.arange(groups + 1)[:, None, None]
    state_at = jnp.arange(groups)[None, :, None]
    step_at = jnp.arange(groups)[None, None, :]
    inside = (carry_at <= step_at) & (step_at < state_at)
    spans = jnp.prod(jnp.where(inside[None], flow.T[:, None, None, :], 1.0), axis=3)
    link_at = jnp.concatenate([linked, jnp.zeros((1,), jnp.float32)])
    coef = (
        jnp.where((carry_at[:, :, 0] <= state_at[:, :, 0])[None], spans, 0.0)
        * link_at[None, :, None]
    )
    carries = jnp.einsum("hcd,dhpn->chpn", coef, states, precision=lax.Precision.HIGHEST)
    start_grad = carries[0]
    end_grads = carries[1:]
    return (
        cum_sums,
        cum_group,
        seg_group,
        alive_group,
        last_label,
        grad_group,
        end_grads,
        start_grad,
    )


def group_output(key_rows, queries, parts):
    cum_sums, cum_group, seg_group, alive_group, last_label, grad_group, end_grads, start_grad = (
        parts
    )
    groups = seg_group.shape[0]
    head_count = cum_group.shape[1]
    key_group = key_rows.reshape(groups, GROUP, N)
    query_group = queries.reshape(groups, GROUP, N)
    scores = jnp.einsum("csn,ctn->cst", query_group, key_group, preferred_element_type=jnp.float32)
    row_index = lax.broadcasted_iota(jnp.int32, (GROUP, GROUP), 0)
    col_index = lax.broadcasted_iota(jnp.int32, (GROUP, GROUP), 1)
    keep_mask = (
        (row_index >= col_index)[None]
        & (seg_group[:, :, None] == seg_group[:, None, :])
        & alive_group[:, :, None]
    )
    spread = cum_group[:, :, :, None] - cum_group[:, :, None, :]
    decays = jnp.exp(jnp.where(keep_mask[:, None], spread, -jnp.inf))
    mixing = (scores[:, None] * decays).astype(jnp.bfloat16)
    inner_part = jnp.einsum(
        "chst,cshp->cthp", mixing, grad_group, preferred_element_type=jnp.float32
    )
    across = jnp.einsum(
        "chpn,ctn->cthp",
        end_grads.astype(jnp.bfloat16),
        key_group,
        preferred_element_type=jnp.float32,
    )
    reach_weight = jnp.where(
        (seg_group == last_label[:, None])[:, None, :],
        jnp.exp(cum_group[:, :, -1:] - cum_group),
        0.0,
    )
    summed_parts = inner_part + across * reach_weight.transpose(0, 2, 1)[:, :, :, None]
    return summed_parts.reshape(groups * GROUP, head_count * P_SIZE)


def initial_state(out_grad, queries, decay, segment, alive_mask, cum_sums):
    tokens = out_grad.shape[0]
    head_count = decay.shape[0]
    firsts = jnp.concatenate([jnp.ones((1,), jnp.bool_), segment[1:] != segment[:-1]])
    labels = jnp.arange(RESP_DEV + 1, dtype=jnp.int32)
    member = segment[:, None] == labels[None, :]
    opening = cum_sums - decay
    base_label = jnp.sum(
        jnp.where((member & firsts[:, None])[None], opening[:, :, None], 0.0), axis=1
    )
    base_token = jnp.sum(jnp.where(member[None], base_label[:, None, :], 0.0), axis=2)
    factor = jnp.where(alive_mask[None], jnp.exp(cum_sums - base_token), 0.0)
    weighted = (factor.T[:, :, None] * out_grad.reshape(tokens, head_count, P_SIZE)).astype(
        jnp.bfloat16
    )
    return jnp.einsum("thp,tn->hpn", weighted, queries, preferred_element_type=jnp.float32)


def on_device(
    prompt_grad,
    prompt_keys,
    prompt_queries,
    prompt_decay,
    resp_grad,
    resp_keys,
    resp_queries,
    resp_decay,
    resp_segment,
):
    resp_alive = resp_segment < RESP_DEV
    resp_parts = group_parts(resp_grad, resp_queries, resp_decay, resp_segment, resp_alive)
    resp_dx = group_output(resp_keys, resp_queries, resp_parts).astype(jnp.bfloat16)
    partial_state = initial_state(
        resp_grad, resp_queries, resp_decay, resp_segment, resp_alive, resp_parts[0]
    )
    summed_state = lax.psum(partial_state, "resp")
    head_count = prompt_decay.shape[0]
    prompt_len = prompt_grad.shape[0]
    zero_label = jnp.zeros((prompt_len,), jnp.int32)
    all_alive = jnp.ones((prompt_len,), jnp.bool_)
    prompt_parts = group_parts(prompt_grad, prompt_queries, prompt_decay, zero_label, all_alive)
    cum_sums = prompt_parts[0]
    start_grad = prompt_parts[7]
    shard_total = cum_sums[:, -1]
    seq_index = lax.axis_index("seq")
    resp_index = lax.axis_index("resp")
    first_head = seq_index * summed_state.shape[0]
    owned = first_head // head_count == resp_index
    slots = lax.dynamic_update_slice_in_dim(
        jnp.zeros((head_count,) + summed_state.shape[1:], jnp.float32),
        summed_state,
        first_head % head_count,
        0,
    )
    my_heads = lax.psum(jnp.where(owned, slots, 0.0), "seq")
    span_len = lax.axis_size("seq")
    whole_b = start_grad
    whole_a = jnp.exp(shard_total)
    later_b = jnp.zeros_like(start_grad)
    later_a = jnp.ones_like(whole_a)
    shift = 1
    while shift < span_len:
        pairs = [(k + shift, k) for k in range(span_len - shift)]
        message = jnp.concatenate(
            [whole_b, jnp.broadcast_to(whole_a[:, None, None], (head_count, 1, N))], axis=1
        )
        got = lax.ppermute(message, "seq", pairs)
        valid = seq_index + shift < span_len
        got_b = jnp.where(valid, got[:, :P_SIZE], 0.0)
        got_a = jnp.where(valid, got[:, P_SIZE, 0], 1.0)
        later_b = later_b + later_a[:, None, None] * got_b
        later_a = later_a * got_a
        if shift * 2 < span_len:
            whole_b = whole_b + whole_a[:, None, None] * got_b
            whole_a = whole_a * got_a
        shift *= 2
    incoming = later_b + later_a[:, None, None] * my_heads
    local_part = group_output(prompt_keys, prompt_queries, prompt_parts)
    carry_term = jnp.einsum(
        "hpn,tn->thp",
        incoming.astype(jnp.bfloat16),
        prompt_keys,
        preferred_element_type=jnp.float32,
    )
    carry_term = carry_term * jnp.exp(shard_total[:, None] - cum_sums).T[:, :, None]
    prompt_dx = (local_part + carry_term.reshape(prompt_len, head_count * P_SIZE)).astype(
        jnp.bfloat16
    )
    return (prompt_dx, resp_dx)


def solution(mesh):
    return jax.shard_map(
        on_device,
        mesh=mesh,
        in_specs=(
            P("seq", "resp"),
            P("seq", None),
            P("seq", None),
            P("resp", "seq"),
            P("resp", "seq"),
            P("resp", None),
            P("resp", None),
            P("seq", "resp"),
            P("resp"),
        ),
        out_specs=(P("seq", "resp"), P("resp", "seq")),
        check_vma=False,
    )
```

profile of v0, /device:TPU:1, one launch (start us, length us, event | category | flops | bytes accessed | tf_op | source)
XLA Modules:
  0.0 240.0 jit_solution(917676850013422105)
XLA Ops:
  7.3 0.9 copy.104
  8.2 2.3 reduce-window.14
  11.2 1.0 copy.111
  14.4 0.8 reshape.320
  17.5 3.8 %convolution_bitcast_fusion = f32[5,8,64,128]{3,0,2,1:T(8,128)} fusion(f32[8,5,4,1]{1,2,3,0:T(4,128)S(1)} %copy.138, f32[4,8,64,128]{3,2,1,0:T(8,128)S(1)} %fusion.28), kind=kOutput, calls=%fused_computation.29 | convolution fusion | flops 15728640 | bytes 2359936 | tf_op jit(solution)/shard_map/hcd,dhpn->chpn/dot_general | solution.py:50
  21.4 1.8 slice.133
  23.2 0.7 pad_maximum_fusion
  24.0 5.1 %collective-permute-start = (f32[8,65,128]{2,1,0:T(8,128)}, f32[8,65,128]{2,1,0:T(8,128)}, u32[]{:S(2)}, u32[]{:S(2)}) collective-permute-start(f32[8,65,128]{2,1,0:T(8,128)} %pad_maximum_fusion), channel_id=1, source_target_pairs={{8,0},{16,8},{24,16},{32,24},{40,32},{48,40},{56,48},{64,56},{72,6... | collective-permute-start | bytes 798728 | tf_op jit(solution)/shard_map/ppermute | solution.py:168
  29.2 2.4 copy.120
  32.9 1.3 reduce-window.16
  34.7 1.3 fusion.96
  36.1 2.3 fusion.20
  38.4 2.7 %slice.252 = bf16[4,8,64,128]{3,0,2,1:T(4,128)(2,1)} slice(f32[5,8,64,128]{3,0,2,1:T(8,128)} %convolution_bitcast_fusion), slice={[1:5], [0:8], [0:64], [0:128]} | slice | bytes 1048576 | tf_op jit(solution)/shard_map/slice | solution.py:52
  44.1 0.8 reduce_window_sum.43
  45.5 0.8 copy.121
  47.7 2.4 %copy.156 = bf16[16,8,16,256]{3,2,1,0:T(8,128)(2,1)} copy(bf16[16,8,16,256]{3,1,2,0:T(8,128)(2,1)} %bitcast.176) | data formatting | bytes 2097152
  50.2 0.8 copy.127
  52.6 2.7 %and_and_fusion = pred[16,256,256]{2,1,0:T(8,128)(4,1)S(1)} fusion(s32[16,256]{1,0:T(8,128)S(1)} %eq.84, pred[16,256]{1,0:T(8,128)(4,1)S(1)} %and.103, pred[256,256]{1,0:T(8,128)(4,1)} %iota_compare_fusion.1), kind=kLoop, calls=%fused_computation.15 | loop fusion | flops 3145728 | bytes 1134592 | tf_op jit(solution)/shard_map/and | solution.py:77
  56.8 1.5 fusion.33
  59.7 3.6 %fusion.18 = f32[4,256,8,64]{1,3,2,0:T(8,128)} fusion(f32[4,8,64,256]{3,2,1,0:T(8,128)S(1)} %fusion.33, f32[4,8,256]{2,1,0:T(8,128)S(1)} %copy-done.20, f32[4,256,256]{2,1,0:T(8,128)S(1)} %fusion.97, pred[256,256]{1,0:T(8,128)(4,1)S(1)} %copy-done.17, bf16[4,256,8,64]{1,0,3,2:T(4,128)(2,1)S(1)} %reshape.320, f32[4,256,8]{1,2,0:T(8,128)S(1)} %copy-done.18), kind=kOutput, calls=%fused_computation.26 | convolution fusion | flops 277872640 | bytes 6422528 | tf_op jit(solution)/shard_map/chst,cshp->cthp/dot_general | solution.py:84
  63.3 3.8 %fusion.3 = f32[16,2,256,64]{2,3,1,0:T(8,128)} fusion(f32[16,2,256]{2,1,0:T(2,128)S(1)} %bitcast.201, f32[16,256,256]{2,1,0:T(8,128)S(1)} %fusion.98, pred[16,256,256]{2,1,0:T(8,128)(4,1)S(1)} %and_and_fusion, bf16[16,256,2,64]{1,0,3,2:T(8,128)(2,1)S(1)} %bitcast.177), kind=kOutput, calls=%fused_computation.5 | convolution fusion | flops 276824064 | bytes 8421376 | tf_op jit(solution)/shard_map/chst,cshp->cthp/dot_general | solution.py:84
  67.4 0.9 fusion.93
  68.3 1.0 multiply_add_fusion.3
  69.4 1.5 collective-permute-start.1
  71.5 8.5 %collective-permute-done.1 = f32[8,65,128]{2,1,0:T(8,128)S(1)} collective-permute-done((f32[8,65,128]{2,1,0:T(8,128)S(1)}, f32[8,65,128]{2,1,0:T(8,128)S(1)}, u32[]{:S(2)}, u32[]{:S(2)}) %collective-permute-start.1) | collective-permute-done | bytes 266272 | tf_op jit(solution)/shard_map/ppermute | solution.py:168
  80.0 0.9 multiply_reduce_fusion.2
  81.1 0.7 pad_maximum_fusion.2
  81.9 1.4 collective-permute-start.2
  83.3 2.0 fusion.19
  85.3 1.0 slice.153
  86.3 7.6 %collective-permute-done.2 = f32[8,65,128]{2,1,0:T(8,128)} collective-permute-done((f32[8,65,128]{2,1,0:T(8,128)}, f32[8,65,128]{2,1,0:T(8,128)}, u32[]{:S(2)}, u32[]{:S(2)}) %collective-permute-start.2) | collective-permute-done | bytes 266272 | tf_op jit(solution)/shard_map/ppermute | solution.py:168
  93.9 0.9 fusion.89
  94.8 1.0 multiply_add_fusion.1
  96.0 1.3 collective-permute-start.3
  97.3 2.5 %fusion.16 = bf16[16,256,2,64]{1,3,2,0:T(8,128)(2,1)} fusion(f32[16,2,256,64]{2,3,1,0:T(8,128)S(1)} %copy-done.6, bf16[16,256,128,1]{2,1,3,0:T(8,128)(2,1)S(1)} %bitcast.170, f32[16,256,2]{1,2,0:T(2,128)S(1)} %get-tuple-element.33, bf16[16,2,64,128]{3,0,2,1:T(8,128)(2,1)} %slice.153), kind=kOutput, calls=%fused_computation.21 | convolution fusion | flops 135790592 | bytes 4751360 | tf_op jit(solution)/shard_map/chpn,ctn->cthp/dot_general | solution.py:87
  99.8 5.5 %collective-permute-done.3 = f32[8,65,128]{2,1,0:T(8,128)S(1)} collective-permute-done((f32[8,65,128]{2,1,0:T(8,128)S(1)}, f32[8,65,128]{2,1,0:T(8,128)S(1)}, u32[]{:S(2)}, u32[]{:S(2)}) %collective-permute-start.3) | collective-permute-done | bytes 266272 | tf_op jit(solution)/shard_map/ppermute | solution.py:168
  105.6 0.7 pad_maximum_fusion.4
  106.4 1.3 collective-permute-start.4
  107.8 0.9 select_dynamic-update-slice_fusion
  109.5 2.9 %copy.117 = f32[4,256,8,64]{1,0,3,2:T(4,128)S(1)} copy(f32[4,256,8,64]{1,3,2,0:T(8,128)} %fusion.18) | data formatting | bytes 4194304 | tf_op jit(solution)/shard_map/add | solution.py:98
  112.5 1.8 copy.152
  114.3 4.5 %copy.149 = bf16[16,256,2,64]{3,2,1,0:T(2,128)(2,1)S(1)} copy(bf16[16,256,2,64]{1,3,2,0:T(8,128)(2,1)} %fusion.16) | data formatting | bytes 2097152
  118.8 1.8 reshape.341
  120.6 1.1 multiply_reduce_fusion.1
  121.7 105.9 %all-reduce.5.cloned.1.call-done = f32[8,64,128]{2,1,0:T(8,128)} async-done(((f32[8,64,128]{2,1,0:T(8,128)}), f32[8,64,128]{2,1,0:T(8,128)}) %all-reduce.5.cloned.1.call-update) | async-done | bytes 262160 | tf_op jit(solution)/shard_map/psum | solution.py:156
  227.6 1.9 bitcast_multiply_fusion.1
  229.4 1.4 fusion.17
  230.9 2.3 copy.135
  (129 shorter events, 19.2 us)
Async XLA Ops:
  7.2 51.5 %copy-start = (bf16[4096,128]{1,0:T(8,128)(2,1)S(1)}, bf16[4096,128]{1,0:T(8,128)(2,1)}, u32[]{:S(2)}) copy-start(bf16[4096,128]{1,0:T(8,128)(2,1)} %param.14) | copy-start | bytes 3145732
  7.2 6.7 %copy-start.7 = (bf16[1024,512]{1,0:T(8,128)(2,1)S(1)}, bf16[1024,512]{1,0:T(8,128)(2,1)}, u32[]{:S(2)}) copy-start(bf16[1024,512]{1,0:T(8,128)(2,1)} %param.9) | copy-start | bytes 3145732
  7.2 100.6 %all-reduce.3.cloned.1.call-start = ((), (), s32[]{:S(2)}) async-start(), calls=%async_computation | async-start | bytes 131072 | tf_op jit(solution)/shard_map/psum | solution.py:137
  10.9 5.0 %copy-start.15 = (f32[1,8,8,128]{3,2,1,0:T(8,128)}, f32[1,8,8,128]{3,2,1,0:T(8,128)S(1)}, u32[]{:S(2)}) copy-start(f32[1,8,8,128]{3,2,1,0:T(8,128)S(1)} %fusion.109) | copy-start | bytes 98308
  14.4 2.7 %copy-start.8 = (bf16[1024,128]{1,0:T(8,128)(2,1)S(1)}, bf16[1024,128]{1,0:T(8,128)(2,1)}, u32[]{:S(2)}) copy-start(bf16[1024,128]{1,0:T(8,128)(2,1)} %param.11) | copy-start | bytes 786436
  17.5 11.6 %copy-start.13 = (s32[4096]{0:T(1024)S(1)}, s32[4096]{0:T(1024)}, u32[]{:S(2)}) copy-start(s32[4096]{0:T(1024)} %param.17) | copy-start | bytes 49156
  21.4 11.0 %copy-start.14 = (f32[2,4096]{1,0:T(2,128)S(1)}, f32[2,4096]{1,0:T(2,128)}, u32[]{:S(2)}) copy-start(f32[2,4096]{1,0:T(2,128)} %param.16) | copy-start | bytes 98308
  24.0 43.4 %collective-permute-start = (f32[8,65,128]{2,1,0:T(8,128)}, f32[8,65,128]{2,1,0:T(8,128)}, u32[]{:S(2)}, u32[]{:S(2)}) collective-permute-start(f32[8,65,128]{2,1,0:T(8,128)} %pad_maximum_fusion), channel_id=1, source_target_pairs={{8,0},{16,8},{24,16},{32,24},{40,32},{48,40},{56,48},{64,56},{72,6... | collective-permute-start | bytes 798728 | tf_op jit(solution)/shard_map/ppermute | solution.py:168
  29.2 6.9 %copy-start.2 = (bf16[4096,128]{1,0:T(8,128)(2,1)S(1)}, bf16[4096,128]{1,0:T(8,128)(2,1)}, u32[]{:S(2)}) copy-start(bf16[4096,128]{1,0:T(8,128)(2,1)} %param.15) | copy-start | bytes 3145732
  38.4 189.2 %all-reduce.5.cloned.1.call-start = ((), (), s32[]{:S(2)}) async-start(), calls=%async_computation.1 | async-start | bytes 524288 | tf_op jit(solution)/shard_map/psum | solution.py:156
  43.9 11.3 %copy-start.21 = (f32[15]{0:T(128)}, f32[15]{0:T(128)S(1)}, u32[]{:S(2)}) copy-start(f32[15]{0:T(128)S(1)} %convert_reduce_fusion) | copy-start | bytes 184
  52.6 5.8 %copy-start.4 = (bf16[1024,128]{1,0:T(8,128)(2,1)S(1)}, bf16[1024,128]{1,0:T(8,128)(2,1)}, u32[]{:S(2)}) copy-start(bf16[1024,128]{1,0:T(8,128)(2,1)} %param.10) | copy-start | bytes 786436
  52.6 5.8 %copy-start.9 = (bf16[1024,128]{1,0:T(8,128)(2,1)S(1)}, bf16[1024,128]{1,0:T(8,128)(2,1)}, u32[]{:S(2)}) copy-start(bf16[1024,128]{1,0:T(8,128)(2,1)} %param.11) | copy-start | bytes 786436
  58.7 1.0 copy-start.17
  58.7 1.0 copy-start.18
  58.7 1.0 copy-start.20
  59.7 3.7 %copy-start.3 = (bf16[16,8,16,256]{3,2,1,0:T(8,128)(2,1)S(1)}, bf16[16,8,16,256]{3,2,1,0:T(8,128)(2,1)}, u32[]{:S(2)}) copy-start(bf16[16,8,16,256]{3,2,1,0:T(8,128)(2,1)} %copy.156) | copy-start | bytes 3145732
  59.7 3.7 %copy-start.19 = (f32[2,16,256]{2,0,1:T(2,128)S(1)}, f32[2,16,256]{2,0,1:T(2,128)}, u32[]{:S(2)}) copy-start(f32[2,16,256]{2,0,1:T(2,128)} %copy.189) | copy-start | bytes 98308
  67.2 1.1 copy-start.22
  69.4 10.6 %collective-permute-start.1 = (f32[8,65,128]{2,1,0:T(8,128)S(1)}, f32[8,65,128]{2,1,0:T(8,128)S(1)}, u32[]{:S(2)}, u32[]{:S(2)}) collective-permute-start(f32[8,65,128]{2,1,0:T(8,128)S(1)} %pad_maximum_fusion.1), channel_id=1, source_target_pairs={{16,0},{24,8},{32,16},{40,24},{48,32},{56,40},{64,48},{72,56},{80,... | collective-permute-start | bytes 798728 | tf_op jit(solution)/shard_map/ppermute | solution.py:168
  80.0 5.2 %copy-start.11 = (f32[8,65,128]{2,1,0:T(8,128)}, f32[8,65,128]{2,1,0:T(8,128)S(1)}, u32[]{:S(2)}) copy-start(f32[8,65,128]{2,1,0:T(8,128)S(1)} %collective-permute-done.1) | copy-start | bytes 798724
  81.9 15.4 %copy-start.6 = (f32[16,2,256,64]{2,3,1,0:T(8,128)S(1)}, f32[16,2,256,64]{2,3,1,0:T(8,128)}, u32[]{:S(2)}) copy-start(f32[16,2,256,64]{2,3,1,0:T(8,128)} %fusion.3) | copy-start | bytes 6291460
  81.9 12.0 %collective-permute-start.2 = (f32[8,65,128]{2,1,0:T(8,128)}, f32[8,65,128]{2,1,0:T(8,128)}, u32[]{:S(2)}, u32[]{:S(2)}) collective-permute-start(f32[8,65,128]{2,1,0:T(8,128)} %pad_maximum_fusion.2), channel_id=1, source_target_pairs={{32,0},{40,8},{48,16},{56,24},{64,32},{72,40},{80,48},{88,56},{96,... | collective-permute-start | bytes 798728 | tf_op jit(solution)/shard_map/ppermute | solution.py:168
  96.0 9.3 %collective-permute-start.3 = (f32[8,65,128]{2,1,0:T(8,128)S(1)}, f32[8,65,128]{2,1,0:T(8,128)S(1)}, u32[]{:S(2)}, u32[]{:S(2)}) collective-permute-start(f32[8,65,128]{2,1,0:T(8,128)S(1)} %pad_maximum_fusion.3), channel_id=1, source_target_pairs={{64,0},{72,8},{80,16},{88,24},{96,32},{104,40},{112,48},{120,56},{... | collective-permute-start | bytes 798728 | tf_op jit(solution)/shard_map/ppermute | solution.py:168
  97.3 12.1 %copy-start.16 = (f32[1,8,8,128]{3,2,1,0:T(8,128)S(1)}, f32[1,8,8,128]{3,2,1,0:T(8,128)}, u32[]{:S(2)}) copy-start(f32[1,8,8,128]{3,2,1,0:T(8,128)} %copy-done.15) | copy-start | bytes 98308
  105.3 1.1 copy-start.12
  106.4 14.3 %collective-permute-start.4 = (f32[8,65,128]{2,1,0:T(8,128)}, f32[8,65,128]{2,1,0:T(8,128)}, u32[]{:S(2)}, u32[]{:S(2)}) collective-permute-start(f32[8,65,128]{2,1,0:T(8,128)} %pad_maximum_fusion.4), channel_id=1, source_target_pairs={{128,0},{136,8},{144,16},{152,24},{160,32},{168,40},{176,48},{184,... | collective-permute-start | bytes 798728 | tf_op jit(solution)/shard_map/ppermute | solution.py:168
  108.7 0.7 copy-start.10
  118.8 108.7 %copy-start.5 = (bf16[1024,128]{1,0:T(8,128)(2,1)S(1)}, bf16[1024,128]{1,0:T(8,128)(2,1)}, u32[]{:S(2)}) copy-start(bf16[1024,128]{1,0:T(8,128)(2,1)} %param.10) | copy-start | bytes 786436
  120.6 108.8 %copy-start.1 = (f32[64,8,4,256]{3,1,2,0:T(8,128)S(1)}, f32[64,8,4,256]{3,1,2,0:T(8,128)}, u32[]{:S(2)}) copy-start(f32[64,8,4,256]{3,1,2,0:T(8,128)} %copy.152) | copy-start | bytes 6291460
Sparse Core Ops, SparseCore 0:
  38.5 69.2 all-reduce.2
  111.0 116.4 all-reduce.4
where the time goes:
time: 241 us; the launch traced here: 240 us
  waiting for transfers between devices  128 us (53%)
  local copies, waits for them, and re-layouts  36.5 us (15%)
  other arithmetic  27.1 us (11%)
  matrix products  23.4 us (10%)
  between operations  14.6 us (6%)
  starting transfers between devices  10.6 us (4%)
    psum x1, waiting for transfers between devices, on_device(): my_heads = lax.psum(jnp.where(owned, slots, 0.0), 'seq')  106 us
    ppermute x5, waiting for transfers between devices, on_device(): got = lax.ppermute(message, 'seq', pairs)  21.7 us
    unnamed x57, local copies, waits for them, and re-layouts  17.3 us
    ppermute x5, starting transfers between devices, on_device(): got = lax.ppermute(message, 'seq', pairs)  10.6 us
    dot_general x2, matrix products, group_output(): jnp.einsum('chst,cshp->cthp', mixing, grad_group, preferred_element_type=...  7.47 us
    dot_general x2, matrix products, group_parts(): jnp.einsum('hcd,dhpn->chpn', coef, states, precision=lax.Precision.HIGHEST)  5.81 us
  transfers between devices with their start and end apart: 7, of which 5 were waited for; matrix products, arithmetic and copies ran while one was open for 27% of the time, Pallas kernels for 0%

commit v1 on v0

--- a/solution.py
+++ b/solution.py
@@ -153,7 +153,9 @@
         first_head % head_count,
         0,
     )
-    my_heads = lax.psum(jnp.where(owned, slots, 0.0), "seq")
+    part = jnp.where(owned, slots, 0.0)
+    terms = lax.all_gather(part, "seq")
+    my_heads = jnp.sum(terms, axis=0)
     span_len = lax.axis_size("seq")
     whole_b = start_grad
     whole_a = jnp.exp(shard_total)

time: 241 us -> 212 us (0.88)
  the two profiles are of different devices: /device:TPU:1 before, /device:TPU:30 now
where the time goes in v1:
time: 212 us; the launch traced here: 211 us
  waiting for transfers between devices  92.5 us (44%)
  local copies, waits for them, and re-layouts  36.2 us (17%)
  other arithmetic  26.2 us (12%)
  starting transfers between devices  22.4 us (11%)
  matrix products  18.7 us (9%)
  between operations  14.7 us (7%)
    psum x1, waiting for transfers between devices, on_device(): summed_state = lax.psum(partial_state, 'resp')  75.1 us
    ppermute x5, starting transfers between devices, on_device(): got = lax.ppermute(message, 'seq', pairs)  22.3 us
    unnamed x81, local copies, waits for them, and re-layouts  18.7 us
    ppermute x5, waiting for transfers between devices, on_device(): got = lax.ppermute(message, 'seq', pairs)  17.3 us
    dot_general x2, matrix products, group_output(): jnp.einsum('chst,cshp->cthp', mixing, grad_group, preferred_element_type=...  7.54 us
    dot_general x2, matrix products, group_parts(): jnp.einsum('hcd,dhpn->chpn', coef, states, precision=lax.Precision.HIGHEST)  4.49 us
  transfers between devices with their start and end apart: 7, of which 4 were waited for; matrix products, arithmetic and copies ran while one was open for 29% of the time, Pallas kernels for 0%

profile of v1, /device:TPU:30, one launch (start us, length us, event | category | flops | bytes accessed | tf_op | source)
XLA Modules:
  0.0 210.7 jit_solution(11274825924101678788)
XLA Ops:
  7.2 0.8 broadcast_compare_fusion.1
  8.0 0.9 slice_compare_fusion
  8.9 0.8 copy.222
  10.7 0.9 bitcast_subtract_fusion.1
  11.6 0.8 iota_compare_fusion
  12.4 1.5 copy.155
  14.4 1.1 fusion.20
  15.6 75.1 %all-reduce.2.cloned.1.call-done = f32[2,64,128]{2,1,0:T(8,128)} async-done(((f32[2,64,128]{2,1,0:T(8,128)}), f32[2,64,128]{2,1,0:T(8,128)}) %all-reduce.2.cloned.1.call-update) | async-done | bytes 65552 | tf_op jit(solution)/shard_map/psum | solution.py:137
  91.5 2.3 %reduce-window.14 = f32[8,8,128]{2,1,0:T(8,128)S(1)} reduce-window(f32[8,8,128]{2,1,0:T(8,128)S(1)} %copy.139, f32[]{:T(128)} %constant.29.clone.1), window={size=1x1x128 pad=0_0x0_0x127_0}, to_apply=%region_0.0 | reduce-window | flops 1040384 | bytes 65540 | tf_op jit(solution)/shard_map/reduce-window
  94.4 1.0 copy.140
  95.4 1.0 copy.146
  96.5 0.8 multiply_bitcast_fusion.1
  99.0 2.3 %copy.143 = bf16[1024,512]{0,1:T(8,128)(2,1)} copy(bf16[1024,512]{1,0:T(8,128)(2,1)} %param.9) | data formatting | bytes 2097152 | tf_op args[0]
  101.2 2.7 %reshape.322 = bf16[4,256,8,64]{1,0,3,2:T(4,128)(2,1)} reshape(bf16[1024,512]{0,1:T(8,128)(2,1)} %copy.143) | data formatting | bytes 2097152 | tf_op jit(solution)/shard_map/reshape | solution.py:24
  103.9 1.7 multiply_convert_fusion.5
  106.0 2.5 %convolution_bitcast_fusion = f32[5,8,64,128]{3,0,2,1:T(8,128)S(1)} fusion(f32[8,5,4,1]{1,2,3,0:T(4,128)S(1)} %copy.173, f32[4,8,64,128]{3,2,1,0:T(8,128)S(1)} %fusion.28), kind=kOutput, calls=%fused_computation.29 | convolution fusion | flops 15728640 | bytes 2359936 | tf_op jit(solution)/shard_map/hcd,dhpn->chpn/dot_general | solution.py:50
  108.6 1.4 copy-done.6
  110.8 0.8 pad_maximum_fusion
  111.5 1.9 collective-permute-start
  114.2 0.8 reduce_window_sum.43
  115.6 0.8 copy.156
  116.4 2.7 %slice.252 = bf16[4,8,64,128]{3,0,2,1:T(4,128)(2,1)} slice(f32[5,8,64,128]{3,0,2,1:T(8,128)} %copy-done.6), slice={[1:5], [0:8], [0:64], [0:128]} | slice | bytes 1048576 | tf_op jit(solution)/shard_map/slice | solution.py:52
  120.4 1.6 copy.162
  126.9 1.4 and_and_fusion
  129.6 3.7 %fusion.18 = f32[4,256,8,64]{1,3,2,0:T(8,128)} fusion(f32[4,8,64,256]{3,2,1,0:T(8,128)S(1)} %fusion.33, f32[4,8,256]{2,1,0:T(8,128)S(1)} %copy-done.26, f32[4,256,256]{2,1,0:T(8,128)S(1)} %fusion.97, pred[256,256]{1,0:T(8,128)(4,1)S(1)} %iota_compare_fusion.1, bf16[4,256,8,64]{1,0,3,2:T(4,128)(2,1)S(1)} %copy-done.5, f32[4,256,8]{1,2,0:T(8,128)S(1)} %copy-done.24), kind=kOutput, calls=%fused_computation.26 | convolution fusion | flops 277872640 | bytes 6422528 | tf_op jit(solution)/shard_map/chst,cshp->cthp/dot_general | solution.py:84
  133.3 3.9 %fusion.3 = f32[16,2,256,64]{2,3,1,0:T(8,128)} fusion(f32[16,2,256]{2,1,0:T(2,128)S(1)} %bitcast.203, f32[16,256,256]{2,1,0:T(8,128)S(1)} %fusion.98, pred[16,256,256]{2,1,0:T(8,128)(4,1)S(1)} %and_and_fusion, bf16[16,256,2,64]{1,0,3,2:T(8,128)(2,1)S(1)} %bitcast.179), kind=kOutput, calls=%fused_computation.5 | convolution fusion | flops 276824064 | bytes 8421376 | tf_op jit(solution)/shard_map/chst,cshp->cthp/dot_general | solution.py:84
  137.3 1.1 fusion.93
  138.5 1.0 multiply_add_fusion.3
  139.6 2.7 %collective-permute-start.1 = (f32[8,65,128]{2,1,0:T(8,128)S(1)}, f32[8,65,128]{2,1,0:T(8,128)S(1)}, u32[]{:S(2)}, u32[]{:S(2)}) collective-permute-start(f32[8,65,128]{2,1,0:T(8,128)S(1)} %pad_maximum_fusion.1), channel_id=1, source_target_pairs={{16,0},{24,8},{32,16},{40,24},{48,32},{56,40},{64,48},{72,56},{80,... | collective-permute-start | bytes 798728 | tf_op jit(solution)/shard_map/ppermute | solution.py:170
  142.6 8.7 %collective-permute-done.1 = f32[8,65,128]{2,1,0:T(8,128)S(1)} collective-permute-done((f32[8,65,128]{2,1,0:T(8,128)S(1)}, f32[8,65,128]{2,1,0:T(8,128)S(1)}, u32[]{:S(2)}, u32[]{:S(2)}) %collective-permute-start.1) | collective-permute-done | bytes 266272 | tf_op jit(solution)/shard_map/ppermute | solution.py:170
  151.3 0.9 multiply_reduce_fusion.2
  152.4 5.5 %collective-permute-start.2 = (f32[8,65,128]{2,1,0:T(8,128)S(1)}, f32[8,65,128]{2,1,0:T(8,128)S(1)}, u32[]{:S(2)}, u32[]{:S(2)}) collective-permute-start(f32[8,65,128]{2,1,0:T(8,128)S(1)} %pad_maximum_fusion.2), channel_id=1, source_target_pairs={{32,0},{40,8},{48,16},{56,24},{64,32},{72,40},{80,48},{88,56},{96,... | collective-permute-start | bytes 798728 | tf_op jit(solution)/shard_map/ppermute | solution.py:170
  158.5 5.6 %collective-permute-done.2 = f32[8,65,128]{2,1,0:T(8,128)S(1)} collective-permute-done((f32[8,65,128]{2,1,0:T(8,128)S(1)}, f32[8,65,128]{2,1,0:T(8,128)S(1)}, u32[]{:S(2)}, u32[]{:S(2)}) %collective-permute-start.2) | collective-permute-done | bytes 266272 | tf_op jit(solution)/shard_map/ppermute | solution.py:170
  164.1 0.9 fusion.89
  165.2 5.7 %collective-permute-start.3 = (f32[8,65,128]{2,1,0:T(8,128)S(1)}, f32[8,65,128]{2,1,0:T(8,128)S(1)}, u32[]{:S(2)}, u32[]{:S(2)}) collective-permute-start(f32[8,65,128]{2,1,0:T(8,128)S(1)} %pad_maximum_fusion.3), channel_id=1, source_target_pairs={{64,0},{72,8},{80,16},{88,24},{96,32},{104,40},{112,48},{120,56},{... | collective-permute-start | bytes 798728 | tf_op jit(solution)/shard_map/ppermute | solution.py:170
  171.0 2.0 fusion.19
  173.2 3.0 %collective-permute-done.3 = f32[8,65,128]{2,1,0:T(8,128)S(1)} collective-permute-done((f32[8,65,128]{2,1,0:T(8,128)S(1)}, f32[8,65,128]{2,1,0:T(8,128)S(1)}, u32[]{:S(2)}, u32[]{:S(2)}) %collective-permute-start.3) | collective-permute-done | bytes 266272 | tf_op jit(solution)/shard_map/ppermute | solution.py:170
  176.5 0.7 pad_maximum_fusion.4
  177.3 6.4 %collective-permute-start.4 = (f32[8,65,128]{2,1,0:T(8,128)}, f32[8,65,128]{2,1,0:T(8,128)}, u32[]{:S(2)}, u32[]{:S(2)}) collective-permute-start(f32[8,65,128]{2,1,0:T(8,128)} %pad_maximum_fusion.4), channel_id=1, source_target_pairs={{128,0},{136,8},{144,16},{152,24},{160,32},{168,40},{176,48},{184,... | collective-permute-start | bytes 798728 | tf_op jit(solution)/shard_map/ppermute | solution.py:170
  183.7 1.5 fusion.16
  185.6 1.4 copy.152
  187.0 1.9 copy.187
  188.8 4.5 %copy.184 = bf16[16,256,2,64]{3,2,1,0:T(2,128)(2,1)S(1)} copy(bf16[16,256,2,64]{1,3,2,0:T(8,128)(2,1)} %fusion.16) | data formatting | bytes 2097152
  193.4 1.8 reshape.343
  195.3 0.9 multiply_reduce_fusion.1
  196.2 4.0 %reduce_sum.29 = f32[8,64,128]{2,1,0:T(8,128)S(1)} reduce(f32[32,8,64,128]{3,2,1,0:T(8,128)} %all-gather.2.cloned.1.call-done, f32[]{:T(128)} %constant.29.clone.1), dimensions={0}, to_apply=%region_8.9 | reduce | flops 2031616 | bytes 8650756 | tf_op jit(solution)/shard_map/reduce_sum | solution.py:158
  200.3 1.7 bitcast_multiply_fusion.1
  202.5 1.3 copy.170
  (154 shorter events, 17.7 us)
Async XLA Ops:
  7.2 121.1 %copy-start = (bf16[4096,128]{1,0:T(8,128)(2,1)S(1)}, bf16[4096,128]{1,0:T(8,128)(2,1)}, u32[]{:S(2)}) copy-start(bf16[4096,128]{1,0:T(8,128)(2,1)} %param.14) | copy-start | bytes 3145732
  7.2 83.5 %all-reduce.2.cloned.1.call-start = ((), (), s32[]{:S(2)}) async-start(), calls=%async_computation | async-start | bytes 131072 | tf_op jit(solution)/shard_map/psum | solution.py:137
  10.6 3.8 %copy-start.2 = (bf16[4096,128]{1,0:T(8,128)(2,1)S(1)}, bf16[4096,128]{1,0:T(8,128)(2,1)}, u32[]{:S(2)}) copy-start(bf16[4096,128]{1,0:T(8,128)(2,1)} %param.15) | copy-start | bytes 3145732
  13.9 77.5 %copy-start.23 = (f32[8,1024]{1,0:T(8,128)S(1)}, f32[8,1024]{1,0:T(8,128)}, u32[]{:S(2)}) copy-start(f32[8,1024]{1,0:T(8,128)} %param.12) | copy-start | bytes 98308
  14.4 82.0 %copy-start.34 = (f32[4]{0:T(128)S(1)}, f32[4]{0:T(128)}, u32[]{:S(2)}) copy-start(f32[4]{0:T(128)} %constant.54.clone.1) | copy-start | bytes 52
  14.4 82.9 %copy-start.32 = (f32[5]{0:T(128)S(1)}, f32[5]{0:T(128)}, u32[]{:S(2)}) copy-start(f32[5]{0:T(128)} %constant.56.clone.1) | copy-start | bytes 64
  15.5 180.7 %all-gather.2.cloned.1.call-start = ((), (), s32[]{:S(2)}) async-start(), calls=%async_computation.1 | async-start | bytes 8650752 | tf_op jit(solution)/shard_map/all_gather | solution.py:157
  90.7 0.7 copy-start.14
  94.2 4.7 %copy-start.21 = (f32[1,8,8,128]{3,2,1,0:T(8,128)}, f32[1,8,8,128]{3,2,1,0:T(8,128)S(1)}, u32[]{:S(2)}) copy-start(f32[1,8,8,128]{3,2,1,0:T(8,128)S(1)} %fusion.109) | copy-start | bytes 98308
  94.4 15.8 %copy-start.28 = (f32[8,1]{0,1:T(1,128)}, f32[8,1]{0,1:T(1,128)S(1)}, u32[]{:S(2)}) copy-start(f32[8,1]{0,1:T(1,128)S(1)} %copy.186) | copy-start | bytes 100
  101.2 4.4 %copy-start.12 = (bf16[1024,128]{1,0:T(8,128)(2,1)S(1)}, bf16[1024,128]{1,0:T(8,128)(2,1)}, u32[]{:S(2)}) copy-start(bf16[1024,128]{1,0:T(8,128)(2,1)} %param.11) | copy-start | bytes 786436
  106.0 7.5 %copy-start.19 = (s32[4096]{0:T(1024)S(1)}, s32[4096]{0:T(1024)}, u32[]{:S(2)}) copy-start(s32[4096]{0:T(1024)} %param.17) | copy-start | bytes 49156
  108.6 1.4 copy-start.6
  110.0 9.2 %copy-start.20 = (f32[2,4096]{1,0:T(2,128)S(1)}, f32[2,4096]{1,0:T(2,128)}, u32[]{:S(2)}) copy-start(f32[2,4096]{1,0:T(2,128)} %param.16) | copy-start | bytes 98308
  111.5 25.8 %collective-permute-start = (f32[8,65,128]{2,1,0:T(8,128)}, f32[8,65,128]{2,1,0:T(8,128)}, u32[]{:S(2)}, u32[]{:S(2)}) collective-permute-start(f32[8,65,128]{2,1,0:T(8,128)} %pad_maximum_fusion), channel_id=1, source_target_pairs={{8,0},{16,8},{24,16},{32,24},{40,32},{48,40},{56,48},{64,56},{72,6... | collective-permute-start | bytes 798728 | tf_op jit(solution)/shard_map/ppermute | solution.py:170
  122.9 0.5 copy-start.30
  125.1 0.8 copy-start.27
  125.1 1.0 copy-start.7
  125.1 1.0 copy-start.13
  125.1 1.3 copy-start.11
  125.3 7.9 %copy-start.3 = (bf16[16,8,16,256]{3,2,1,0:T(8,128)(2,1)}, bf16[16,8,16,256]{3,2,1,0:T(8,128)(2,1)S(1)}, u32[]{:S(2)}) copy-start(bf16[16,8,16,256]{3,2,1,0:T(8,128)(2,1)S(1)} %copy.191) | copy-start | bytes 3145732
  128.3 1.3 copy-start.5
  128.3 1.2 copy-start.24
  128.3 1.2 copy-start.26
  129.6 3.7 %copy-start.25 = (f32[2,16,256]{2,0,1:T(2,128)S(1)}, f32[2,16,256]{2,0,1:T(2,128)}, u32[]{:S(2)}) copy-start(f32[2,16,256]{2,0,1:T(2,128)} %copy.224) | copy-start | bytes 98308
  133.3 3.9 %copy-start.31 = (f32[15]{0:T(128)S(1)}, f32[15]{0:T(128)}, u32[]{:S(2)}) copy-start(f32[15]{0:T(128)} %copy-done.30) | copy-start | bytes 184
  133.3 4.0 %copy-start.33 = (f32[8,1,1]{0,2,1:T(1,128)S(1)}, f32[8,1,1]{0,2,1:T(1,128)}, u32[]{:S(2)}) copy-start(f32[8,1,1]{0,2,1:T(1,128)} %get-tuple-element.43) | copy-start | bytes 100
  133.3 4.0 %copy-start.29 = (f32[8,1]{0,1:T(1,128)S(1)}, f32[8,1]{0,1:T(1,128)}, u32[]{:S(2)}) copy-start(f32[8,1]{0,1:T(1,128)} %copy-done.28) | copy-start | bytes 100
  137.1 5.2 %copy-start.4 = (bf16[16,8,16,256]{3,2,1,0:T(8,128)(2,1)S(1)}, bf16[16,8,16,256]{3,2,1,0:T(8,128)(2,1)}, u32[]{:S(2)}) copy-start(bf16[16,8,16,256]{3,2,1,0:T(8,128)(2,1)} %copy-done.3) | copy-start | bytes 3145732
  139.6 11.7 %collective-permute-start.1 = (f32[8,65,128]{2,1,0:T(8,128)S(1)}, f32[8,65,128]{2,1,0:T(8,128)S(1)}, u32[]{:S(2)}, u32[]{:S(2)}) collective-permute-start(f32[8,65,128]{2,1,0:T(8,128)S(1)} %pad_maximum_fusion.1), channel_id=1, source_target_pairs={{16,0},{24,8},{32,16},{40,24},{48,32},{56,40},{64,48},{72,56},{80,... | collective-permute-start | bytes 798728 | tf_op jit(solution)/shard_map/ppermute | solution.py:170
  152.4 11.7 %collective-permute-start.2 = (f32[8,65,128]{2,1,0:T(8,128)S(1)}, f32[8,65,128]{2,1,0:T(8,128)S(1)}, u32[]{:S(2)}, u32[]{:S(2)}) collective-permute-start(f32[8,65,128]{2,1,0:T(8,128)S(1)} %pad_maximum_fusion.2), channel_id=1, source_target_pairs={{32,0},{40,8},{48,16},{56,24},{64,32},{72,40},{80,48},{88,56},{96,... | collective-permute-start | bytes 798728 | tf_op jit(solution)/shard_map/ppermute | solution.py:170
  164.1 9.1 %copy-start.17 = (f32[8,65,128]{2,1,0:T(8,128)}, f32[8,65,128]{2,1,0:T(8,128)S(1)}, u32[]{:S(2)}) copy-start(f32[8,65,128]{2,1,0:T(8,128)S(1)} %collective-permute-done.2) | copy-start | bytes 798724
  165.2 18.5 %copy-start.9 = (f32[16,2,256,64]{2,3,1,0:T(8,128)S(1)}, f32[16,2,256,64]{2,3,1,0:T(8,128)}, u32[]{:S(2)}) copy-start(f32[16,2,256,64]{2,3,1,0:T(8,128)} %fusion.3) | copy-start | bytes 6291460
  165.2 11.0 %collective-permute-start.3 = (f32[8,65,128]{2,1,0:T(8,128)S(1)}, f32[8,65,128]{2,1,0:T(8,128)S(1)}, u32[]{:S(2)}, u32[]{:S(2)}) collective-permute-start(f32[8,65,128]{2,1,0:T(8,128)S(1)} %pad_maximum_fusion.3), channel_id=1, source_target_pairs={{64,0},{72,8},{80,16},{88,24},{96,32},{104,40},{112,48},{120,56},{... | collective-permute-start | bytes 798728 | tf_op jit(solution)/shard_map/ppermute | solution.py:170
  176.2 7.5 %copy-start.15 = (f32[8,65,128]{2,1,0:T(8,128)}, f32[8,65,128]{2,1,0:T(8,128)S(1)}, u32[]{:S(2)}) copy-start(f32[8,65,128]{2,1,0:T(8,128)S(1)} %collective-permute-done.3) | copy-start | bytes 798724
  177.3 18.0 %collective-permute-start.4 = (f32[8,65,128]{2,1,0:T(8,128)}, f32[8,65,128]{2,1,0:T(8,128)}, u32[]{:S(2)}, u32[]{:S(2)}) collective-permute-start(f32[8,65,128]{2,1,0:T(8,128)} %pad_maximum_fusion.4), channel_id=1, source_target_pairs={{128,0},{136,8},{144,16},{152,24},{160,32},{168,40},{176,48},{184,... | collective-permute-start | bytes 798728 | tf_op jit(solution)/shard_map/ppermute | solution.py:170
  183.7 1.9 copy-start.10
  193.4 1.8 copy-start.22
  196.2 4.1 %copy-start.8 = (bf16[1024,128]{1,0:T(8,128)(2,1)S(1)}, bf16[1024,128]{1,0:T(8,128)(2,1)}, u32[]{:S(2)}) copy-start(bf16[1024,128]{1,0:T(8,128)(2,1)} %param.10) | copy-start | bytes 786436
  196.2 4.1 %copy-start.16 = (f32[8,65,128]{2,1,0:T(8,128)S(1)}, f32[8,65,128]{2,1,0:T(8,128)}, u32[]{:S(2)}) copy-start(f32[8,65,128]{2,1,0:T(8,128)} %copy-done.15) | copy-start | bytes 798724
  196.2 4.1 %copy-start.18 = (f32[8,65,128]{2,1,0:T(8,128)S(1)}, f32[8,65,128]{2,1,0:T(8,128)}, u32[]{:S(2)}) copy-start(f32[8,65,128]{2,1,0:T(8,128)} %copy-done.17) | copy-start | bytes 798724
  200.3 1.8 copy-start.1
Sparse Core Ops, SparseCore 0:
  15.6 74.9 all-reduce.1
  93.2 54.8 all-gather.1
